TPU v7x, 256 devices: a whole 4x4x8 slice. The times are simulated.
256 devices in a mesh: row: 16 (over z_lo, y), col: 8 (over x, core), layer: 2 (over z_hi).
Axes of the slice: x: 4, y: 4, z: 8 (z_hi: 2, z_lo: 4; z = z_hi * 4 + z_lo), core: 2. Of those that a mesh axis runs over, the one named last changes fastest.
Arguments:
- density: float32 [2, 8192, 2048], P('layer', 'row', 'col'), may hold values from -6 to 6
- dens_mask: int32 [2, 128, 32], P('layer', 'row', 'col'), may hold values from 0 to 1, as said below
- hamiltonian: float32 [2, 2048, 16384], P('layer', 'row', 'col'), may hold values from -0.375 to 0.375
- ham_mask: int32 [2, 32, 256], P('layer', None, 'col'), may hold values from 0 to 1, as said below
- filter_mask: int32 [128, 256], P('row', 'col'), may hold values from 0 to 1, as said below
Outputs:
- product: float32 [8192, 16384], P('row', ('col', 'layer'))
Inputs may be any that keep to these rules, and one draw needn't show every extreme that they name: `dens_mask`: 1 where a density block is nonzero, else 0. `ham_mask`: 1 where a Hamiltonian block is nonzero, else 0. `filter_mask`: 1 where a result block is kept, else 0.
All inputs are finite; a program needn't handle non-finite values.
Results may differ from a plain program's by a relative error of at most 0.0001.
Values sent between devices are 32-bit elements; how exact they have to be, the bound alone decides.
No kernel may reach another device: no remote copies, remote signals or barrier semaphores. Data moves between devices by JAX's collectives and lax.ppermute only.
A program may use at most 128 MiB of HBM per device.

v0:
```python
import jax
import jax.numpy as jnp
from jax import lax
from jax.sharding import PartitionSpec as P

BLOCK = 64


def expand(block_mask):
    widened = jnp.repeat(block_mask.astype(jnp.float32), BLOCK, axis=-2)
    return jnp.repeat(widened, BLOCK, axis=-1)


def shards(density, dens_mask, hamiltonian, ham_mask, filter_mask):
    dens_vals = density * expand(dens_mask)
    ham_count = hamiltonian.shape[1]
    row_ids = lax.axis_index("row") * ham_count + jnp.arange(ham_count, dtype=jnp.int32)
    block_ids = row_ids // BLOCK
    one_hot = (
        block_ids[:, None] == jnp.arange(ham_mask.shape[1], dtype=jnp.int32)[None, :]
    ).astype(jnp.float32)
    picked = jnp.dot(
        one_hot,
        ham_mask[0].astype(jnp.float32),
        precision=lax.Precision.HIGHEST,
        preferred_element_type=jnp.float32,
    )
    ham_vals = hamiltonian * jnp.repeat(picked, BLOCK, axis=1)[None]
    kept = expand(filter_mask)
    ham_group = lax.all_gather(ham_vals, "row", axis=1, tiled=True)
    ham_part = ham_group[0]
    partial_value = jnp.dot(
        lax.all_gather(dens_vals, "col", axis=2, tiled=True)[0],
        ham_part,
        precision=lax.Precision.HIGHEST,
        preferred_element_type=jnp.float32,
    )
    return lax.psum_scatter(partial_value * kept, "layer", scatter_dimension=1, tiled=True)


def solution(mesh):
    return jax.shard_map(
        shards,
        mesh=mesh,
        in_specs=(
            P("layer", "row", "col"),
            P("layer", "row", "col"),
            P("layer", "row", "col"),
            P("layer", None, "col"),
            P("row", "col"),
        ),
        out_specs=P("row", ("col", "layer")),
        check_vma=False,
    )
```

profile of v0, /device:TPU:1, one launch (start us, length us, event | category | flops | bytes accessed | tf_op | source)
XLA Modules:
  0.0 426.2 jit_solution(16033029685912236478)
XLA Ops:
  6.5 0.0 copy-start.1
  6.5 0.0 copy-start
  6.5 0.0 all-gather.3.cloned.1.call-start
  6.5 1.3 copy.8
  7.8 0.7 convert_bitcast_fusion
  8.5 0.1 broadcast_in_dim.21
  8.6 0.1 broadcast_in_dim.22
  8.7 0.9 bitcast_multiply_fusion.1
  9.5 0.0 all-gather.3.cloned.1.call-update
  9.6 0.0 all-gather.5.cloned.1.call-start
  9.6 1.6 copy.9
  11.2 0.0 copy-done.1
  11.2 0.2 fusion.8
  11.4 1.1 bitcast_multiply_fusion
  12.5 0.0 all-gather.5.cloned.1.call-update
  12.5 0.0 reduce-scatter.2.cloned.1.call-start
  12.6 0.0 copy-done
  12.6 0.1 copy.10
  12.7 0.1 broadcast_in_dim.26
  12.8 0.1 reshape.35
  12.9 2.5 broadcast_in_dim.27
  15.4 5.5 %copy.11 = f32[512,2048]{1,0:T(8,128)} copy(f32[512,2048]{0,1:T(8,128)} %bitcast.24) | data formatting | bytes 8388608 | tf_op jit(solution)/shard_map/reshape | solution.py:11
  20.8 27.6 %all-gather.3.cloned.1.call-done = f32[1,512,2048]{1,2,0:T(8,128)} async-done(((f32[1,512,256]{1,2,0:T(8,128)}), f32[1,512,2048]{1,2,0:T(8,128)}) %all-gather.3.cloned.1.call-update) | async-done | bytes 4194320 | tf_op jit(solution)/shard_map/all_gather | solution.py:33
  48.5 194.2 %all-gather.5.cloned.1.call-done = f32[1,2048,2048]{1,2,0:T(8,128)} async-done(((f32[1,128,2048]{1,2,0:T(8,128)}), f32[1,2048,2048]{1,2,0:T(8,128)}) %all-gather.5.cloned.1.call-update) | async-done | bytes 16777232 | tf_op jit(solution)/shard_map/all_gather | solution.py:30
  242.7 57.7 %fusion.3 = f32[512,2048]{1,0:T(8,128)} fusion(f32[512,2048]{1,0:T(8,128)} %copy.11, f32[1,2048,2048]{1,2,0:T(8,128)} %all-gather.5.cloned.1.call-done, f32[1,512,2048]{1,2,0:T(8,128)} %all-gather.3.cloned.1.call-done), kind=kOutput, calls=%fused_computation.3 | convolution fusion | flops 25770852352 | bytes 29360128 | tf_op jit(solution)/shard_map/dot_general | solution.py:32
  300.3 0.0 reduce-scatter.2.cloned.1.call-update
  300.3 119.4 %reduce-scatter.2.cloned.1.call-done = f32[512,1024]{1,0:T(8,128)} async-done(((f32[512,2048]{1,0:T(8,128)}), f32[512,1024]{1,0:T(8,128)}) %reduce-scatter.2.cloned.1.call-update) | async-done | bytes 2097168 | tf_op jit(solution)/shard_map/reduce_scatter | solution.py:38
  (2 shorter events, 0.0 us)
Async XLA Ops:
  6.5 4.7 %copy-start.1 = (s32[1,32,32]{2,1,0:T(8,128)S(1)}, s32[1,32,32]{2,1,0:T(8,128)}, u32[]{:S(2)}) copy-start(s32[1,32,32]{2,1,0:T(8,128)} %param.8) | copy-start | bytes 12292
  6.5 6.1 %copy-start = (s32[8,32]{1,0:T(8,128)S(1)}, s32[8,32]{1,0:T(8,128)}, u32[]{:S(2)}) copy-start(s32[8,32]{1,0:T(8,128)} %param.9) | copy-start | bytes 3076
  6.5 41.9 %all-gather.3.cloned.1.call-start = ((), (), s32[]{:S(2)}) async-start(), calls=%async_computation.1 | async-start | bytes 4718592 | tf_op jit(solution)/shard_map/all_gather | solution.py:33
  9.6 233.1 %all-gather.5.cloned.1.call-start = ((), (), s32[]{:S(2)}) async-start(), calls=%async_computation.2 | async-start | bytes 17825792 | tf_op jit(solution)/shard_map/all_gather | solution.py:30
  12.5 407.2 %reduce-scatter.2.cloned.1.call-start = ((), (), s32[]{:S(2)}) async-start(), calls=%async_computation.3 | async-start | bytes 6291456 | tf_op jit(solution)/shard_map/reduce_scatter | solution.py:38
Sparse Core Ops, SparseCore 0:
  9.7 38.7 all-gather.2
  50.2 192.4 all-gather.4
  300.5 119.2 reduce-scatter.1
where the time goes:
time: 426 us
  waiting for transfers between devices  341 us (80%)
  matrix products  57.9 us (14%)
  between operations  13.2 us (3%)
  local copies, waits for them, and re-layouts  11.2 us (3%)
    all_gather x1, waiting for transfers between devices, shards(): ham_group = lax.all_gather(ham_vals, 'row', axis=1, tiled=True)  194 us
    reduce_scatter x1, waiting for transfers between devices, shards(): lax.psum_scatter(partial_value * kept, 'layer', scatter_dimension=1, tile...  119 us
    dot_general x1, matrix products, shards(): jnp.dot(lax.all_gather(dens_vals, 'col', axis=2, tiled=True)[0], ham_part...  57.7 us
    all_gather x1, waiting for transfers between devices, shards(): lax.all_gather(dens_vals, 'col', axis=2, tiled=True)[0]  27.6 us
  transfers between devices with their start and end apart: 3, of which 3 were waited for; matrix products, arithmetic and copies ran while one was open for 3% of the time, Pallas kernels for 0%

commit v1 on v0

--- a/solution.py
+++ b/solution.py
@@ -30,7 +30,9 @@
     ham_group = lax.all_gather(ham_vals, "row", axis=1, tiled=True)
     ham_part = ham_group[0]
     partial_value = jnp.dot(
-        lax.all_gather(dens_vals, "col", axis=2, tiled=True)[0],
+        jnp.concatenate(
+            lax.all_to_all(jnp.stack([dens_vals] * lax.axis_size("col")), "col", 0, 0), axis=2
+        )[0],
         ham_part,
         precision=lax.Precision.HIGHEST,
         preferred_element_type=jnp.float32,

time: 426 us -> 391 us (0.918)
  waiting for transfers between devices: 341 us -> 297 us
  starting transfers between devices: 0.09 us -> 7.78 us
    all_gather x1, waiting for transfers between devices: 194 us -> 137 us  [shards(): ham_group = lax.all_gather(ham_vals, 'row', axis=1, tiled=True)]
    all_to_all x0 -> x1, waiting for transfers between devices: none -> 40.6 us  [shards(): lax.all_to_all(jnp.stack([dens_vals] * lax.axis_size('col')), 'col', 0, 0)]
    all_gather x1 -> x0, waiting for transfers between devices: 27.6 us -> none  [shards(): lax.all_gather(dens_vals, 'col', axis=2, tiled=True)[0]]
    all_to_all x0 -> x1, starting transfers between devices: none -> 7.77 us  [shards(): lax.all_to_all(jnp.stack([dens_vals] * lax.axis_size('col')), 'col', 0, 0)]
where the time goes in v1:
time: 391 us
  waiting for transfers between devices  297 us (76%)
  matrix products  58.6 us (15%)
  between operations  13.5 us (3%)
  local copies, waits for them, and re-layouts  12.7 us (3%)
  starting transfers between devices  7.78 us (2%)
    all_gather x1, waiting for transfers between devices, shards(): ham_group = lax.all_gather(ham_vals, 'row', axis=1, tiled=True)  137 us
    reduce_scatter x1, waiting for transfers between devices, shards(): lax.psum_scatter(partial_value * kept, 'layer', scatter_dimension=1, tile...  119 us
    dot_general x1, matrix products, shards(): jnp.dot(jnp.concatenate(lax.all_to_all(jnp.stack([dens_vals] * lax.axis_s...  57.6 us
    all_to_all x1, waiting for transfers between devices, shards(): lax.all_to_all(jnp.stack([dens_vals] * lax.axis_size('col')), 'col', 0, 0)  40.6 us
  transfers between devices with their start and end apart: 3, of which 3 were waited for; matrix products, arithmetic and copies ran while one was open for 3% of the time, Pallas kernels for 0%

profile of v1, /device:TPU:1, one launch (start us, length us, event | category | flops | bytes accessed | tf_op | source)
XLA Modules:
  0.0 390.9 jit_solution(1963832733471518998)
XLA Ops:
  6.5 0.0 copy-start
  6.5 0.0 copy-start.2
  6.5 0.0 all-gather.2.cloned.1.call-start
  6.5 1.6 copy.14
  8.2 0.9 fusion.5
  9.1 1.1 bitcast_multiply_fusion
  10.2 0.0 all-gather.2.cloned.1.call-update
  10.2 0.0 copy-done
  10.2 0.2 copy.12
  10.4 0.0 copy-done.2
  10.5 0.1 broadcast_in_dim.21
  10.5 0.1 broadcast_in_dim.22
  10.6 0.1 bitcast_multiply_fusion.1
  10.7 2.5 stack.2
  13.2 0.0 copy-start.1
  13.2 7.8 %all-to-all-start = ((f32[8,1,512,256]{2,3,1,0:T(8,128)}), f32[8,1,512,256]{2,3,1,0:T(8,128)}, u32[]{:S(2)}, u32[]{:S(2)}) async-start(f32[8,1,512,256]{2,3,1,0:T(8,128)} %stack.2), calls=%async_computation | async-start | bytes 8388608 | tf_op jit(solution)/shard_map/all_to_all | solution.py:34
  21.0 0.0 reduce-scatter.2.cloned.1.call-start
  21.0 0.0 copy-done.1
  21.0 0.1 copy.15
  21.1 0.1 broadcast_in_dim.26
  21.2 0.1 reshape.42
  21.3 2.5 broadcast_in_dim.27
  23.7 5.5 %copy.16 = f32[512,2048]{1,0:T(8,128)} copy(f32[512,2048]{0,1:T(8,128)} %bitcast.26) | data formatting | bytes 8388608 | tf_op jit(solution)/shard_map/reshape | solution.py:11
  29.2 40.6 %all-to-all-done = f32[8,1,512,256]{2,3,1,0:T(8,128)} async-done(((f32[8,1,512,256]{2,3,1,0:T(8,128)}), f32[8,1,512,256]{2,3,1,0:T(8,128)}, u32[]{:S(2)}, u32[]{:S(2)}) %all-to-all-start) | async-done | bytes 4194336 | tf_op jit(solution)/shard_map/all_to_all | solution.py:34
  69.8 137.2 %all-gather.2.cloned.1.call-done = f32[1,2048,2048]{1,2,0:T(8,128)} async-done(((f32[1,128,2048]{1,2,0:T(8,128)}), f32[1,2048,2048]{1,2,0:T(8,128)}) %all-gather.2.cloned.1.call-update) | async-done | bytes 16777232 | tf_op jit(solution)/shard_map/all_gather | solution.py:30
  207.0 57.6 %fusion.2 = f32[512,2048]{1,0:T(8,128)} fusion(f32[512,2048]{1,0:T(8,128)} %copy.16, f32[512,2048]{0,1:T(8,128)} %bitcast.5, f32[1,2048,2048]{1,2,0:T(8,128)} %all-gather.2.cloned.1.call-done), kind=kOutput, calls=%fused_computation.2 | convolution fusion | flops 25770852352 | bytes 29360128 | tf_op jit(solution)/shard_map/dot_general | solution.py:32
  264.6 0.0 reduce-scatter.2.cloned.1.call-update
  264.7 119.4 %reduce-scatter.2.cloned.1.call-done = f32[512,1024]{1,0:T(8,128)} async-done(((f32[512,2048]{1,0:T(8,128)}), f32[512,1024]{1,0:T(8,128)}) %reduce-scatter.2.cloned.1.call-update) | async-done | bytes 2097168 | tf_op jit(solution)/shard_map/reduce_scatter | solution.py:40
  (3 shorter events, 0.0 us)
Async XLA Ops:
  6.5 3.7 copy-start
  6.5 3.9 copy-start.2
  6.5 200.5 %all-gather.2.cloned.1.call-start = ((), (), s32[]{:S(2)}) async-start(), calls=%async_computation.2 | async-start | bytes 17825792 | tf_op jit(solution)/shard_map/all_gather | solution.py:30
  13.2 7.8 %copy-start.1 = (s32[8,32]{1,0:T(8,128)S(1)}, s32[8,32]{1,0:T(8,128)}, u32[]{:S(2)}) copy-start(s32[8,32]{1,0:T(8,128)} %param.9) | copy-start | bytes 3076
  13.2 56.6 %all-to-all-start = ((f32[8,1,512,256]{2,3,1,0:T(8,128)}), f32[8,1,512,256]{2,3,1,0:T(8,128)}, u32[]{:S(2)}, u32[]{:S(2)}) async-start(f32[8,1,512,256]{2,3,1,0:T(8,128)} %stack.2), calls=%async_computation | async-start | bytes 8388608 | tf_op jit(solution)/shard_map/all_to_all | solution.py:34
  21.0 363.1 %reduce-scatter.2.cloned.1.call-start = ((), (), s32[]{:S(2)}) async-start(), calls=%async_computation.3 | async-start | bytes 6291456 | tf_op jit(solution)/shard_map/reduce_scatter | solution.py:40
Sparse Core Ops, SparseCore 0:
  10.3 196.6 all-gather.1
  264.8 119.2 reduce-scatter.1
